TPU v7x, 256 devices: a whole 4x4x8 slice. The times are simulated.
256 devices in a mesh: dp: 2 (over z_lo), expert: 32 (over y, z_hi, core), tensor: 4 (over x).
Axes of the slice: x: 4, y: 4, z: 8 (z_hi: 4, z_lo: 2; z = z_hi * 2 + z_lo), core: 2. Of those that a mesh axis runs over, the one named last changes fastest.
Arguments:
- context: bfloat16 [8192, 2048], P(('dp', 'expert'), 'tensor'), may hold values from -6 to 6
- residual: bfloat16 [8192, 2048], P(('dp', 'expert')), may hold values from -6 to 6
- wo_rows: bfloat16 [2048, 2048], P('tensor'), may hold values from -0.125 to 0.125
- norm_gain: float32 [2048], replicated, may hold values from 0.25 to 1.75
- analyzer_out: bfloat16 [8192, 2048], P(('dp', 'expert'), 'tensor'), may hold values from -6 to 6
- gate_probs: float32 [8192, 6], P(('dp', 'expert')), may hold values from 0.05 to 0.5
- expert_ids: int32 [8192, 6], P(('dp', 'expert')), may hold values from 0 to 63, all different within a row; in each aligned block of 128 rows (0 to 127, 128 to 255, ...) at most 14 rows name the same one
- w_gate_up: bfloat16 [64, 2, 2048, 1408], P('expert', None, 'dp', 'tensor'), may hold values from -0.125 to 0.125
- w_down: bfloat16 [64, 1408, 2048], P('expert', 'tensor', 'dp'), may hold values from -0.15625 to 0.15625
Outputs:
- block_out: bfloat16 [8192, 2048], P(('dp', 'expert'), 'tensor')
- context_grad: bfloat16 [8192, 2048], P(('dp', 'expert'), 'tensor')
- gate_prob_grad: float32 [8192, 6], P(('dp', 'expert'))
- gate_up_grad: bfloat16 [64, 2, 2048, 1408], P('expert', None, 'dp', 'tensor')
- down_grad: bfloat16 [64, 1408, 2048], P('expert', 'tensor', 'dp')
Inputs may be any that keep to these rules, and one draw needn't show every extreme that they name: `expert_ids`: each row names 6 different experts; within each device's rows (aligned blocks of 128 rows) no expert is named more than 14 times, a bound that some block reaches.
All inputs are finite; a program needn't handle non-finite values.
Results may differ from a plain program's by a relative error of at most 0.024.
Values may be sent and summed in bfloat16 or wider, within the bound.
No kernel may reach another device: no remote copies, remote signals or barrier semaphores. Data moves between devices by JAX's collectives and lax.ppermute only.
A program may use at most 128 MiB of HBM per device.

v0:
```python
import jax
import jax.numpy as jnp
from jax import lax
from jax.sharding import PartitionSpec as P

EXPERTS = 64
CAP = 14
NORM_EPS = 1e-06
LOSS_WEIGHT = 0.25


def to_experts(outgoing):
    return lax.all_to_all(outgoing, "expert", split_axis=1, concat_axis=1, tiled=True)


def to_tokens(outgoing):
    return lax.all_to_all(outgoing, "expert", split_axis=1, concat_axis=1, tiled=True)


def weight_terms(arrived, activation, grad_in, d_gate_pre, d_up_pre):
    down_part = jnp.einsum(
        "escf,escd->efd", activation, grad_in, preferred_element_type=jnp.float32
    )
    gate_part = jnp.einsum(
        "escd,escf->edf", arrived, d_gate_pre, preferred_element_type=jnp.float32
    )
    up_part = jnp.einsum("escd,escf->edf", arrived, d_up_pre, preferred_element_type=jnp.float32)
    return (jnp.stack([gate_part, up_part], axis=1), down_part)


def per_device(
    context, residual, wo_rows, norm_gain, analyzer_out, gate_probs, expert_ids, w_gate_up, w_down
):
    tok_count, top_count = expert_ids.shape
    feature_count = residual.shape[1]
    tensor_count = lax.axis_size("tensor")
    expert_ranks = lax.axis_size("expert")
    col_count = feature_count // tensor_count
    col_start = lax.axis_index("tensor") * col_count
    local_experts = w_gate_up.shape[0]
    slot_count = EXPERTS * CAP
    expert_range = jnp.arange(EXPERTS, dtype=jnp.int32)
    slot_order = expert_range % local_experts * expert_ranks + expert_range // local_experts
    gate_up_full, down_full = (
        lax.all_gather(w_gate_up, "dp", axis=2, tiled=True),
        lax.all_gather(w_down, "dp", axis=2, tiled=True),
    )
    partial_attn = jnp.dot(context, wo_rows, preferred_element_type=jnp.float32)
    hidden_in = residual.astype(jnp.float32) + lax.psum(
        partial_attn.astype(jnp.bfloat16), "tensor"
    ).astype(jnp.float32)
    inv_rms = lax.rsqrt(jnp.mean(hidden_in * hidden_in, axis=1, keepdims=True) + NORM_EPS)
    normed = (norm_gain * hidden_in * inv_rms).astype(jnp.bfloat16)
    flat_ids = expert_ids.reshape(-1)
    onehot = (flat_ids[:, None] == expert_range[None, :]).astype(jnp.int32)
    slot_index = jnp.sum((jnp.cumsum(onehot, axis=0) - onehot) * onehot, axis=1)
    expert_slot = jnp.sum(onehot * slot_order[None, :], axis=1)
    dest_row = expert_slot * CAP + slot_index
    sentinel = tok_count * top_count
    row_entry = (
        jnp.full((slot_count,), sentinel, jnp.int32)
        .at[dest_row]
        .set(jnp.arange(sentinel, dtype=jnp.int32))
    )
    row_token = row_entry // top_count
    gate_pad = jnp.concatenate([gate_probs.reshape(-1), jnp.zeros((1,), jnp.float32)])
    row_gate = gate_pad[row_entry]
    normed_pad = jnp.concatenate([normed, jnp.zeros((1, feature_count), jnp.bfloat16)], axis=0)
    outgoing = normed_pad[row_token].reshape(local_experts, expert_ranks, CAP, feature_count)
    arrived = to_experts(outgoing)
    gate_full = gate_up_full[:, 0]
    up_full = gate_up_full[:, 1]
    pre_gate = jnp.einsum("escd,edf->escf", arrived, gate_full, preferred_element_type=jnp.float32)
    pre_up = jnp.einsum("escd,edf->escf", arrived, up_full, preferred_element_type=jnp.float32)
    activation = (jax.nn.silu(pre_gate) * pre_up).astype(jnp.bfloat16)
    partial_out = jnp.einsum(
        "escf,efd->escd", activation, down_full, preferred_element_type=jnp.float32
    )
    summed_out = lax.psum_scatter(
        partial_out.astype(jnp.bfloat16), "tensor", scatter_dimension=3, tiled=True
    )
    returned = to_tokens(summed_out).reshape(slot_count, col_count)
    entry_out = returned[dest_row].reshape(tok_count, top_count, col_count).astype(jnp.float32)
    hidden_cols = lax.dynamic_slice_in_dim(hidden_in, col_start, col_count, 1)
    block_out = (hidden_cols + jnp.sum(gate_probs[:, :, None] * entry_out, axis=1)).astype(
        jnp.bfloat16
    )
    error = (
        LOSS_WEIGHT * (block_out.astype(jnp.float32) - analyzer_out.astype(jnp.float32))
    ).astype(jnp.bfloat16)
    gate_partial = jnp.sum(error.astype(jnp.float32)[:, None, :] * entry_out, axis=2)
    error_full = lax.all_gather(error, "tensor", axis=1, tiled=True)
    error_pad = jnp.concatenate([error_full, jnp.zeros((1, feature_count), jnp.bfloat16)], axis=0)
    grad_slot = (row_gate[:, None] * error_pad[row_token].astype(jnp.float32)).astype(jnp.bfloat16)
    grad_slot = grad_slot.reshape(local_experts, expert_ranks, CAP, feature_count)
    grad_in = to_experts(grad_slot)
    d_act = jnp.einsum("escd,efd->escf", grad_in, down_full, preferred_element_type=jnp.float32)
    sigmoid_pre = jax.nn.sigmoid(pre_gate)
    d_gate_pre = (d_act * pre_up * sigmoid_pre * (1.0 + pre_gate * (1.0 - sigmoid_pre))).astype(
        jnp.bfloat16
    )
    d_up_pre = (d_act * pre_gate * sigmoid_pre).astype(jnp.bfloat16)
    d_entry_part = jnp.einsum(
        "escf,edf->escd", d_gate_pre, gate_full, preferred_element_type=jnp.float32
    )
    d_entry_part = d_entry_part + jnp.einsum(
        "escf,edf->escd", d_up_pre, up_full, preferred_element_type=jnp.float32
    )
    d_entry_sum = lax.psum_scatter(
        d_entry_part.astype(jnp.bfloat16), "tensor", scatter_dimension=3, tiled=True
    )
    d_returned = to_tokens(d_entry_sum).reshape(slot_count, col_count)
    d_normed = jnp.sum(
        d_returned[dest_row].reshape(tok_count, top_count, col_count).astype(jnp.float32), axis=1
    )
    gain_cols = lax.dynamic_slice_in_dim(norm_gain, col_start, col_count, 0)
    scaled = gain_cols * d_normed
    norm_partial = jnp.sum(scaled * hidden_cols, axis=1)
    norm_dots, gate_prob_grad = lax.psum((norm_partial, gate_partial), "tensor")
    cubed = inv_rms * inv_rms * inv_rms
    d_hidden = (
        error.astype(jnp.float32)
        + inv_rms * scaled
        - hidden_cols * cubed * norm_dots[:, None] / feature_count
    ).astype(jnp.bfloat16)
    context_grad = lax.dot_general(
        lax.all_gather(d_hidden, "tensor", axis=1, tiled=True),
        wo_rows,
        (((1,), (1,)), ((), ())),
        preferred_element_type=jnp.float32,
    ).astype(jnp.bfloat16)
    gate_up_part, down_part = weight_terms(arrived, activation, grad_in, d_gate_pre, d_up_pre)
    gate_up_grad, down_grad = (
        lax.psum_scatter(
            gate_up_part.astype(jnp.bfloat16), "dp", scatter_dimension=2, tiled=True
        ).astype(jnp.float32),
        lax.psum_scatter(
            down_part.astype(jnp.bfloat16), "dp", scatter_dimension=2, tiled=True
        ).astype(jnp.float32),
    )
    return (
        block_out,
        context_grad,
        gate_prob_grad,
        gate_up_grad.astype(jnp.bfloat16),
        down_grad.astype(jnp.bfloat16),
    )


def solution(mesh):
    in_specs = (
        P(("dp", "expert"), "tensor"),
        P(("dp", "expert"), None),
        P("tensor", None),
        P(),
        P(("dp", "expert"), "tensor"),
        P(("dp", "expert"), None),
        P(("dp", "expert"), None),
        P("expert", None, "dp", "tensor"),
        P("expert", "tensor", "dp"),
    )
    out_specs = (
        P(("dp", "expert"), "tensor"),
        P(("dp", "expert"), "tensor"),
        P(("dp", "expert"), None),
        P("expert", None, "dp", "tensor"),
        P("expert", "tensor", "dp"),
    )
    return jax.shard_map(
        per_device, mesh=mesh, in_specs=in_specs, out_specs=out_specs, check_vma=False
    )
```

profile of v0, /device:TPU:1, one launch (start us, length us, event | category | flops | bytes accessed | tf_op | source)
XLA Modules:
  0.0 653.3 jit_solution(14605199587444355152)
XLA Ops:
  11.8 3.7 copy.54
  22.3 39.6 %all-reduce.5.cloned.1.call-done = bf16[128,2048]{1,0:T(8,128)(2,1)} async-done(((bf16[128,2048]{1,0:T(8,128)(2,1)}), bf16[128,2048]{1,0:T(8,128)(2,1)}) %all-reduce.5.cloned.1.call-update) | async-done | bytes 524304 | tf_op jit(solution)/shard_map/psum | solution.py:49
  65.5 5.0 gather_fusion
  70.5 6.0 reshape.133
  76.5 7.8 %copy.53 = bf16[2,32,14,2048]{3,0,2,1:T(2,128)(2,1)} copy(bf16[2,32,14,2048]{3,2,1,0:T(8,128)(2,1)} %reshape.133) | data formatting | bytes 7340032 | tf_op jit(solution)/shard_map/reshape | solution.py:69
  84.3 12.4 %all-to-all-start = ((bf16[2,32,14,2048]{3,0,2,1:T(2,128)(2,1)}), bf16[2,32,14,2048]{3,0,2,1:T(2,128)(2,1)}, u32[]{:S(2)}, u32[]{:S(2)}) async-start(bf16[2,32,14,2048]{3,0,2,1:T(2,128)(2,1)} %copy.53), calls=%async_computation | async-start | bytes 7340032 | tf_op jit(solution)/shard_map/all_to_all | solution.py:13
  98.7 109.8 %all-to-all-done = bf16[2,32,14,2048]{3,0,2,1:T(2,128)(2,1)} async-done(((bf16[2,32,14,2048]{3,0,2,1:T(2,128)(2,1)}), bf16[2,32,14,2048]{3,0,2,1:T(2,128)(2,1)}, u32[]{:S(2)}, u32[]{:S(2)}) %all-to-all-start) | async-done | bytes 3670048 | tf_op jit(solution)/shard_map/all_to_all | solution.py:13
  208.5 7.4 %fusion.8 = f32[2,32,14,352]{3,1,2,0:T(8,128)S(1)} fusion(bf16[2,2,2048,352]{2,3,0,1:T(8,128)(2,1)} %all-gather.3.cloned.1.call-done, bf16[2,32,14,2048]{3,0,2,1:T(2,128)(2,1)} %all-to-all-done), kind=kOutput, calls=%fused_computation.23 | convolution fusion | flops 1291845632 | bytes 7815168 | tf_op jit(solution)/shard_map/escd,edf->escf/dot_general | solution.py:73
  217.1 7.7 %multiply_convert_fusion.3 = (bf16[2,32,14,352]{3,1,2,0:T(8,128)(2,1)S(1)}, f32[2,32,14,352]{3,1,2,0:T(8,128)}) fusion(f32[2,32,14,352]{3,1,2,0:T(8,128)S(1)} %fusion.8, bf16[2,2,2048,352]{2,3,0,1:T(8,128)(2,1)S(1)} %copy-done.1, bf16[2,32,14,2048]{3,0,2,1:T(2,128)(2,1)} %all-to-all-done), kind=kOutput, calls=%fused_computation.34 | convolution fusion | flops 1293737984 | bytes 9822208 | tf_op jit(solution)/shard_map/escd,edf->escf/dot_general | solution.py:74
  224.8 5.9 convolution_convert_fusion
  230.8 41.4 %reduce-scatter.5.cloned.1.call-done = bf16[2,32,14,512]{3,1,2,0:T(8,128)(2,1)} async-done(((bf16[2,32,14,2048]{3,1,2,0:T(8,128)(2,1)}), bf16[2,32,14,512]{3,1,2,0:T(8,128)(2,1)}) %reduce-scatter.5.cloned.1.call-update) | async-done | bytes 917520 | tf_op jit(solution)/shard_map/reduce_scatter | solution.py:79
  275.2 10.7 %all-to-all-start.1 = ((bf16[2,32,14,512]{3,0,2,1:T(2,128)(2,1)}), bf16[2,32,14,512]{3,0,2,1:T(2,128)(2,1)S(1)}, u32[]{:S(2)}, u32[]{:S(2)}) async-start(bf16[2,32,14,512]{3,0,2,1:T(2,128)(2,1)} %copy.57), calls=%async_computation.2 | async-start | bytes 1835008 | tf_op jit(solution)/shard_map/all_to_all | solution.py:17
  286.3 3.7 gather_fusion.2
  290.1 21.6 %all-to-all-done.1 = bf16[2,32,14,512]{3,0,2,1:T(2,128)(2,1)S(1)} async-done(((bf16[2,32,14,512]{3,0,2,1:T(2,128)(2,1)}), bf16[2,32,14,512]{3,0,2,1:T(2,128)(2,1)S(1)}, u32[]{:S(2)}, u32[]{:S(2)}) %all-to-all-start.1) | async-done | bytes 917536 | tf_op jit(solution)/shard_map/all_to_all | solution.py:17
  324.2 10.3 %all_gather.14 = bf16[128,2048]{1,0:T(8,128)(2,1)S(1)} all-gather(bf16[128,512]{1,0:T(8,128)(2,1)S(1)} %get-tuple-element.30), channel_id=1, replica_groups=mesh['dp'=2,'expert'=32,'tensor'=4] {'tensor'}, dimensions={1}, use_global_device_ids=true | all-gather | bytes 655360 | tf_op jit(solution)/shard_map/all_gather | solution.py:92
  334.5 5.0 gather_fusion.3
  339.5 6.3 reshape.138
  345.8 3.9 multiply_convert_fusion
  349.7 3.8 copy.60
  353.5 92.5 %all_to_all.20 = bf16[2,32,14,2048]{3,0,2,1:T(2,128)(2,1)S(1)} all-to-all(bf16[2,32,14,2048]{3,0,2,1:T(2,128)(2,1)S(1)} %copy.60), channel_id=1, replica_groups=mesh['dp'=2,'expert'=32,'tensor'=4] {'expert'}, dimensions={1} | all-to-all | bytes 7340032 | tf_op jit(solution)/shard_map/all_to_all | solution.py:13
  446.0 7.9 %multiply_convert_fusion.1 = (bf16[2,32,14,352]{3,1,2,0:T(8,128)(2,1)S(1)}, bf16[2,32,14,352]{3,1,2,0:T(8,128)(2,1)S(1)}) fusion(f32[2,32,14,352]{3,1,2,0:T(8,128)} %copy-done.14, f32[2,32,14,352]{3,1,2,0:T(8,128)} %get-tuple-element.41, bf16[2,352,2048]{2,1,0:T(8,128)(2,1)S(1)} %copy-done.4, bf16[2,32,14,2048]{3,0,2,1:T(2,128)(2,1)S(1)} %all_to_all.20), kind=kOutput, calls=%fused_computation.32 | convolution fusion | flops 1295945728 | bytes 10338304 | tf_op jit(solution)/shard_map/escd,efd->escf/dot_general | solution.py:97
  456.0 4.0 add_convert_fusion
  460.3 6.8 %fusion.4 = bf16[2,1,2048,352]{2,3,0,1:T(8,128)(2,1)S(1)} fusion(bf16[2,32,14,352]{3,1,2,0:T(8,128)(2,1)S(1)} %get-tuple-element.32, bf16[2,32,14,2048]{3,0,2,1:T(2,128)(2,1)} %all-to-all-done), kind=kOutput, calls=%fused_computation.17 | convolution fusion | flops 1293287424 | bytes 7184384 | tf_op jit(solution)/shard_map/escd,escf->edf/dot_general | solution.py:27
  467.2 6.8 %fusion.3 = bf16[2,1,2048,352]{2,3,0,1:T(8,128)(2,1)S(1)} fusion(bf16[2,32,14,352]{3,1,2,0:T(8,128)(2,1)S(1)} %copy-done.9, bf16[2,32,14,2048]{3,0,2,1:T(2,128)(2,1)} %all-to-all-done), kind=kOutput, calls=%fused_computation.16 | convolution fusion | flops 1293287424 | bytes 7184384 | tf_op jit(solution)/shard_map/escd,escf->edf/dot_general | solution.py:24
  478.1 8.3 %bitcast_convert_fusion = bf16[2,352,2048]{2,1,0:T(8,128)(2,1)} fusion(bf16[2,32,14,352]{3,1,2,0:T(8,128)(2,1)S(1)} %copy-done.7, bf16[2,32,14,2048]{3,0,2,1:T(2,128)(2,1)} %copy-done.2), kind=kOutput, calls=%fused_computation.9 | convolution fusion | flops 1293287424 | bytes 7184384 | tf_op jit(solution)/shard_map/escf,escd->efd/dot_general | solution.py:21
  486.4 13.3 %reduce-scatter.7.cloned.1.call-done = bf16[2,32,14,512]{3,1,2,0:T(8,128)(2,1)} async-done(((bf16[2,32,14,2048]{3,1,2,0:T(8,128)(2,1)}), bf16[2,32,14,512]{3,1,2,0:T(8,128)(2,1)}) %reduce-scatter.7.cloned.1.call-update) | async-done | bytes 917520 | tf_op jit(solution)/shard_map/reduce_scatter | solution.py:109
  502.8 10.3 %all-to-all-start.3 = ((bf16[2,32,14,512]{3,0,2,1:T(2,128)(2,1)}), bf16[2,32,14,512]{3,0,2,1:T(2,128)(2,1)S(1)}, u32[]{:S(2)}, u32[]{:S(2)}) async-start(bf16[2,32,14,512]{3,0,2,1:T(2,128)(2,1)} %copy.62), calls=%async_computation.5 | async-start | bytes 1835008 | tf_op jit(solution)/shard_map/all_to_all | solution.py:17
  516.3 33.2 %all-to-all-done.3 = bf16[2,32,14,512]{3,0,2,1:T(2,128)(2,1)S(1)} async-done(((bf16[2,32,14,512]{3,0,2,1:T(2,128)(2,1)}), bf16[2,32,14,512]{3,0,2,1:T(2,128)(2,1)S(1)}, u32[]{:S(2)}, u32[]{:S(2)}) %all-to-all-start.3) | async-done | bytes 917536 | tf_op jit(solution)/shard_map/all_to_all | solution.py:17
  560.7 12.6 %all-reduce.2 = (f32[128]{0:T(128)}, f32[128,6]{1,0:T(8,128)}) all-reduce(f32[128]{0:T(128)S(1)} %multiply_reduce_fusion.3, f32[128,6]{1,0:T(8,128)} %multiply_reduce_fusion), channel_id=1, replica_groups=mesh['dp'=2,'expert'=32,'tensor'=4] {'tensor'}, use_global_device_ids=true, to_apply=%region_12.13 | all-reduce | flops 896 | bytes 7168 | tf_op jit(solution)/shard_map/psum | solution.py:119
  575.6 10.6 %all_gather.15 = bf16[128,2048]{1,0:T(8,128)(2,1)S(1)} all-gather(bf16[128,512]{1,0:T(8,128)(2,1)S(1)} %subtract_convert_fusion), channel_id=1, replica_groups=mesh['dp'=2,'expert'=32,'tensor'=4] {'tensor'}, dimensions={1}, use_global_device_ids=true | all-gather | bytes 655360 | tf_op jit(solution)/shard_map/all_gather | solution.py:127
  587.8 10.1 %reduce-scatter.9.cloned.1.call-done = bf16[2,2,1024,352]{2,3,0,1:T(8,128)(2,1)} async-done(((bf16[2,2,2048,352]{2,3,0,1:T(8,128)(2,1)}), bf16[2,2,1024,352]{2,3,0,1:T(8,128)(2,1)}) %reduce-scatter.9.cloned.1.call-update) | async-done | bytes 2883600 | tf_op jit(solution)/shard_map/reduce_scatter | solution.py:134
  601.6 44.2 %reduce-scatter.11.cloned.1.call-done = bf16[2,352,1024]{2,1,0:T(8,128)(2,1)} async-done(((bf16[2,352,2048]{2,1,0:T(8,128)(2,1)}), bf16[2,352,1024]{2,1,0:T(8,128)(2,1)}) %reduce-scatter.11.cloned.1.call-update) | async-done | bytes 1441808 | tf_op jit(solution)/shard_map/reduce_scatter | solution.py:137
  (99 shorter events, 64.4 us)
Async XLA Ops:
  8.0 1.6 copy-start
  8.0 53.9 %all-reduce.5.cloned.1.call-start = ((), (), s32[]{:S(2)}) async-start(), calls=%async_computation.8 | async-start | bytes 1048576 | tf_op jit(solution)/shard_map/psum | solution.py:49
  11.8 86.9 %all-gather.3.cloned.1.call-start = ((), (), s32[]{:S(2)}) async-start(), calls=%async_computation.9 | async-start | bytes 8650752 | tf_op jit(solution)/shard_map/all_gather | solution.py:45
  15.5 0.7 copy-start.12
  15.5 46.4 %copy-start.5 = (bf16[128,2048]{1,0:T(8,128)(2,1)S(1)}, bf16[128,2048]{1,0:T(8,128)(2,1)}, u32[]{:S(2)}) copy-start(bf16[128,2048]{1,0:T(8,128)(2,1)} %param.10) | copy-start | bytes 1572868
  15.5 47.7 %copy-start.11 = (f32[2048]{0:T(1024)S(1)}, f32[2048]{0:T(1024)}, u32[]{:S(2)}) copy-start(f32[2048]{0:T(1024)} %param.12) | copy-start | bytes 24580
  84.3 124.2 %all-to-all-start = ((bf16[2,32,14,2048]{3,0,2,1:T(2,128)(2,1)}), bf16[2,32,14,2048]{3,0,2,1:T(2,128)(2,1)}, u32[]{:S(2)}, u32[]{:S(2)}) async-start(bf16[2,32,14,2048]{3,0,2,1:T(2,128)(2,1)} %copy.53), calls=%async_computation | async-start | bytes 7340032 | tf_op jit(solution)/shard_map/all_to_all | solution.py:13
  96.8 128.1 %all-gather.5.cloned.1.call-start = ((), (), s32[]{:S(2)}) async-start(), calls=%async_computation.10 | async-start | bytes 4325376 | tf_op jit(solution)/shard_map/all_gather | solution.py:46
  97.3 174.9 %reduce-scatter.5.cloned.1.call-start = ((), (), s32[]{:S(2)}) async-start(), calls=%async_computation.11 | async-start | bytes 4587520 | tf_op jit(solution)/shard_map/reduce_scatter | solution.py:79
  208.5 8.6 %copy-start.1 = (bf16[2,2,2048,352]{2,3,0,1:T(8,128)(2,1)S(1)}, bf16[2,2,2048,352]{2,3,0,1:T(8,128)(2,1)}, u32[]{:S(2)}) copy-start(bf16[2,2,2048,352]{2,3,0,1:T(8,128)(2,1)} %all-gather.3.cloned.1.call-done) | copy-start | bytes 17301508
  215.9 1.2 copy-start.14
  224.8 5.9 copy-start.6
  230.8 55.3 %copy-start.13 = (f32[128,6]{0,1:T(8,128)S(1)}, f32[128,6]{0,1:T(8,128)}, u32[]{:S(2)}) copy-start(f32[128,6]{0,1:T(8,128)} %param.14) | copy-start | bytes 9220
  275.2 36.5 %all-to-all-start.1 = ((bf16[2,32,14,512]{3,0,2,1:T(2,128)(2,1)}), bf16[2,32,14,512]{3,0,2,1:T(2,128)(2,1)S(1)}, u32[]{:S(2)}, u32[]{:S(2)}) async-start(bf16[2,32,14,512]{3,0,2,1:T(2,128)(2,1)} %copy.57), calls=%async_computation.2 | async-start | bytes 1835008 | tf_op jit(solution)/shard_map/all_to_all | solution.py:17
  286.0 213.7 %reduce-scatter.7.cloned.1.call-start = ((), (), s32[]{:S(2)}) async-start(), calls=%async_computation.12 | async-start | bytes 4587520 | tf_op jit(solution)/shard_map/reduce_scatter | solution.py:109
  317.7 4.8 copy-start.10
  353.5 92.5 %copy-start.4 = (bf16[2,352,2048]{2,1,0:T(8,128)(2,1)S(1)}, bf16[2,352,2048]{2,1,0:T(8,128)(2,1)}, u32[]{:S(2)}) copy-start(bf16[2,352,2048]{2,1,0:T(8,128)(2,1)} %all-gather.5.cloned.1.call-done) | copy-start | bytes 8650756
  353.5 100.4 %slice-start = ((s8[5767168]{0:T(1024)(128)(4,1)}), s8[4194304]{0:T(1024)(128)(4,1)S(1)}, s32[]{:S(2)}) async-start(s8[5767168]{0:T(1024)(128)(4,1)} %bitcast.73), calls=%async_computation.15 | async-start | bytes 8388608
  446.0 7.9 %copy-start.2 = (bf16[2,32,14,2048]{3,0,2,1:T(2,128)(2,1)}, bf16[2,32,14,2048]{3,0,2,1:T(2,128)(2,1)S(1)}, u32[]{:S(2)}) copy-start(bf16[2,32,14,2048]{3,0,2,1:T(2,128)(2,1)S(1)} %all_to_all.20) | copy-start | bytes 11010052
  446.0 7.9 %slice-start.1 = ((s8[5767168]{0:T(1024)(128)(4,1)}), s8[1572864]{0:T(1024)(128)(4,1)S(1)}, s32[]{:S(2)}) async-start(s8[5767168]{0:T(1024)(128)(4,1)} %bitcast.73), calls=%async_computation.16 | async-start | bytes 3145728
  453.9 2.1 copy-start.8
  460.1 137.8 %reduce-scatter.9.cloned.1.call-start = ((), (), s32[]{:S(2)}) async-start(), calls=%async_computation.13 | async-start | bytes 8650752 | tf_op jit(solution)/shard_map/reduce_scatter | solution.py:134
  460.3 6.8 %copy-start.9 = (bf16[2,32,14,352]{3,1,2,0:T(8,128)(2,1)S(1)}, bf16[2,32,14,352]{3,1,2,0:T(8,128)(2,1)}, u32[]{:S(2)}) copy-start(bf16[2,32,14,352]{3,1,2,0:T(8,128)(2,1)} %copy-done.8) | copy-start | bytes 1892356
  476.9 1.1 copy-start.7
  477.0 168.7 %reduce-scatter.11.cloned.1.call-start = ((), (), s32[]{:S(2)}) async-start(), calls=%async_computation.14 | async-start | bytes 4325376 | tf_op jit(solution)/shard_map/reduce_scatter | solution.py:137
  502.8 46.7 %all-to-all-start.3 = ((bf16[2,32,14,512]{3,0,2,1:T(2,128)(2,1)}), bf16[2,32,14,512]{3,0,2,1:T(2,128)(2,1)S(1)}, u32[]{:S(2)}, u32[]{:S(2)}) async-start(bf16[2,32,14,512]{3,0,2,1:T(2,128)(2,1)} %copy.62), calls=%async_computation.5 | async-start | bytes 1835008 | tf_op jit(solution)/shard_map/all_to_all | solution.py:17
  555.5 5.0 copy-start.3
Sparse Core Ops, SparseCore 0:
  11.9 49.9 all-reduce.4
  230.9 41.2 reduce-scatter.4
  460.2 39.4 reduce-scatter.6
  502.1 95.7 reduce-scatter.8
  600.8 44.8 reduce-scatter.10
Sparse Core Ops, SparseCore 1:
  15.6 83.0 all-gather.2
  100.3 108.2 all-gather.4
where the time goes:
time: 661 us; the launch traced here: 653 us
  waiting for transfers between devices  315 us (48%)
  blocking collectives  126 us (19%)
  local copies, waits for them, and re-layouts  78.2 us (12%)
  matrix products  60.6 us (9%)
  starting transfers between devices  34.5 us (5%)
  other arithmetic  22.9 us (3%)
  between operations  16.1 us (2%)
    all_to_all x1, waiting for transfers between devices, to_experts(): lax.all_to_all(outgoing, 'expert', split_axis=1, concat_axis=1, tiled=True)  110 us
    all_to_all x1, blocking collectives, to_experts(): lax.all_to_all(outgoing, 'expert', split_axis=1, concat_axis=1, tiled=True)  92.5 us
    all_to_all x2, waiting for transfers between devices, to_tokens(): lax.all_to_all(outgoing, 'expert', split_axis=1, concat_axis=1, tiled=True)  54.9 us
    reduce_scatter x1, waiting for transfers between devices, per_device(): lax.psum_scatter(down_part.astype(jnp.bfloat16), 'dp', scatter_dimension=...  44.2 us
    reduce_scatter x1, waiting for transfers between devices, per_device(): lax.psum_scatter(partial_out.astype(jnp.bfloat16), 'tensor', scatter_dime...  41.4 us
    psum x1, waiting for transfers between devices, per_device(): lax.psum(partial_attn.astype(jnp.bfloat16), 'tensor').astype(jnp.float32)  39.6 us
    all_to_all x2, starting transfers between devices, to_tokens(): lax.all_to_all(outgoing, 'expert', split_axis=1, concat_axis=1, tiled=True)  21.1 us
    reshape x2, local copies, waits for them, and re-layouts, per_device(): normed_pad[row_token]  13.8 us
  transfers between devices with their start and end apart: 10, of which 9 were waited for; matrix products, arithmetic and copies ran while one was open for 15% of the time, Pallas kernels for 0%

commit v1 on v0

--- a/solution.py
+++ b/solution.py
@@ -9,12 +9,19 @@
 LOSS_WEIGHT = 0.25
 
 
+def tiles_define(field):
+    carry_out = jnp.concatenate(
+        lax.all_to_all(jnp.stack(jnp.split(field, lax.axis_size("expert"), 1)), "expert", 0, 0), 1
+    )
+    return carry_out
+
+
 def to_experts(outgoing):
     return lax.all_to_all(outgoing, "expert", split_axis=1, concat_axis=1, tiled=True)
 
 
 def to_tokens(outgoing):
-    return lax.all_to_all(outgoing, "expert", split_axis=1, concat_axis=1, tiled=True)
+    return tiles_define(outgoing)
 
 
 def weight_terms(arrived, activation, grad_in, d_gate_pre, d_up_pre):

time: 661 us -> 670 us (1.014)
    split x0 -> x66, local copies, waits for them, and re-layouts: none -> 10.5 us  [tiles_define(): jnp.split(field, lax.axis_size('expert'), 1)]
  transfers between devices with their start and end apart: 10 -> 10, of which waited for: 9 -> 8; matrix products, arithmetic and copies ran while one was open for 15% -> 15% of each run, Pallas kernels for 0% -> 0%
where the time goes in v1:
time: 670 us; the launch traced here: 662 us
  waiting for transfers between devices  318 us (47%)
  blocking collectives  127 us (19%)
  local copies, waits for them, and re-layouts  82.5 us (12%)
  matrix products  60.6 us (9%)
  starting transfers between devices  34.1 us (5%)
  other arithmetic  22.2 us (3%)
  between operations  17.1 us (3%)
    all_to_all x1, waiting for transfers between devices, to_experts(): lax.all_to_all(outgoing, 'expert', split_axis=1, concat_axis=1, tiled=True)  116 us
    all_to_all x1, blocking collectives, to_experts(): lax.all_to_all(outgoing, 'expert', split_axis=1, concat_axis=1, tiled=True)  92.3 us
    all_to_all x2, waiting for transfers between devices, tiles_define(): lax.all_to_all(jnp.stack(jnp.split(field, lax.axis_size('expert'), 1)), '...  55.7 us
    reduce_scatter x1, waiting for transfers between devices, per_device(): lax.psum_scatter(down_part.astype(jnp.bfloat16), 'dp', scatter_dimension=...  45.4 us
    psum x1, waiting for transfers between devices, per_device(): lax.psum(partial_attn.astype(jnp.bfloat16), 'tensor').astype(jnp.float32)  43.3 us
    reduce_scatter x1, waiting for transfers between devices, per_device(): lax.psum_scatter(partial_out.astype(jnp.bfloat16), 'tensor', scatter_dime...  39.2 us
    all_to_all x2, starting transfers between devices, tiles_define(): lax.all_to_all(jnp.stack(jnp.split(field, lax.axis_size('expert'), 1)), '...  20.7 us
    psum x1, blocking collectives, per_device(): norm_dots, gate_prob_grad = lax.psum((norm_partial, gate_partial), 'tensor')  14 us
  transfers between devices with their start and end apart: 10, of which 8 were waited for; matrix products, arithmetic and copies ran while one was open for 15% of the time, Pallas kernels for 0%

profile of v1, /device:TPU:1, one launch (start us, length us, event | category | flops | bytes accessed | tf_op | source)
XLA Modules:
  0.0 661.7 jit_solution(12023215521845631480)
XLA Ops:
  18.5 43.3 %all-reduce.5.cloned.1.call-done = bf16[128,2048]{1,0:T(8,128)(2,1)} async-done(((bf16[128,2048]{1,0:T(8,128)(2,1)}), bf16[128,2048]{1,0:T(8,128)(2,1)}) %all-reduce.5.cloned.1.call-update) | async-done | bytes 524304 | tf_op jit(solution)/shard_map/psum | solution.py:56
  65.4 5.0 gather_fusion
  70.4 6.0 reshape.133
  76.4 7.8 %copy.3511 = bf16[2,32,14,2048]{3,0,2,1:T(2,128)(2,1)} copy(bf16[2,32,14,2048]{3,2,1,0:T(8,128)(2,1)} %reshape.133) | data formatting | bytes 7340032 | tf_op jit(solution)/shard_map/reshape | solution.py:76
  84.2 12.4 %all-to-all-start = ((bf16[2,32,14,2048]{3,0,2,1:T(2,128)(2,1)}), bf16[2,32,14,2048]{3,0,2,1:T(2,128)(2,1)}, u32[]{:S(2)}, u32[]{:S(2)}) async-start(bf16[2,32,14,2048]{3,0,2,1:T(2,128)(2,1)} %copy.3511), calls=%async_computation | async-start | bytes 7340032 | tf_op jit(solution)/shard_map/all_to_all | solution.py:20
  97.5 115.6 %all-to-all-done = bf16[2,32,14,2048]{3,0,2,1:T(2,128)(2,1)} async-done(((bf16[2,32,14,2048]{3,0,2,1:T(2,128)(2,1)}), bf16[2,32,14,2048]{3,0,2,1:T(2,128)(2,1)}, u32[]{:S(2)}, u32[]{:S(2)}) %all-to-all-start) | async-done | bytes 3670048 | tf_op jit(solution)/shard_map/all_to_all | solution.py:20
  213.1 7.4 %fusion.8 = f32[2,32,14,352]{3,1,2,0:T(8,128)S(1)} fusion(bf16[2,2,2048,352]{2,3,1,0:T(8,128)(2,1)} %all-gather.3.cloned.1.call-done, bf16[2,32,14,2048]{3,0,2,1:T(2,128)(2,1)} %all-to-all-done), kind=kOutput, calls=%fused_computation.23 | convolution fusion | flops 1291845632 | bytes 7815168 | tf_op jit(solution)/shard_map/escd,edf->escf/dot_general | solution.py:80
  221.8 7.7 %multiply_convert_fusion.3 = (bf16[2,32,14,352]{3,1,2,0:T(8,128)(2,1)S(1)}, f32[2,32,14,352]{3,1,2,0:T(8,128)}) fusion(f32[2,32,14,352]{3,1,2,0:T(8,128)S(1)} %fusion.8, bf16[2,2,2048,352]{2,3,1,0:T(8,128)(2,1)S(1)} %copy-done.1, bf16[2,32,14,2048]{3,0,2,1:T(2,128)(2,1)} %all-to-all-done), kind=kOutput, calls=%fused_computation.34 | convolution fusion | flops 1293737984 | bytes 9822208 | tf_op jit(solution)/shard_map/escd,edf->escf/dot_general | solution.py:81
  229.5 5.9 convolution_convert_fusion
  235.5 39.2 %reduce-scatter.5.cloned.1.call-done = bf16[2,32,14,512]{3,1,2,0:T(8,128)(2,1)} async-done(((bf16[2,32,14,2048]{3,1,2,0:T(8,128)(2,1)}), bf16[2,32,14,512]{3,1,2,0:T(8,128)(2,1)}) %reduce-scatter.5.cloned.1.call-update) | async-done | bytes 917520 | tf_op jit(solution)/shard_map/reduce_scatter | solution.py:86
  282.8 10.4 %all-to-all-start.1 = ((bf16[32,2,1,14,512]{4,1,3,2,0:T(2,128)(2,1)}), bf16[32,2,1,14,512]{4,1,3,2,0:T(2,128)(2,1)S(1)}, u32[]{:S(2)}, u32[]{:S(2)}) async-start(bf16[32,2,1,14,512]{4,1,3,2,0:T(2,128)(2,1)} %copy.3576), calls=%async_computation.2 | async-start | bytes 1835008 | tf_op jit(solution)/shard_map/all_to_all | solution.py:14
  293.4 3.7 gather_fusion.2
  297.3 21.6 %all-to-all-done.1 = bf16[32,2,1,14,512]{4,1,3,2,0:T(2,128)(2,1)S(1)} async-done(((bf16[32,2,1,14,512]{4,1,3,2,0:T(2,128)(2,1)}), bf16[32,2,1,14,512]{4,1,3,2,0:T(2,128)(2,1)S(1)}, u32[]{:S(2)}, u32[]{:S(2)}) %all-to-all-start.1) | async-done | bytes 917536 | tf_op jit(solution)/shard_map/all_to_all | solution.py:14
  331.3 10.3 %all_gather.14 = bf16[128,2048]{1,0:T(8,128)(2,1)S(1)} all-gather(bf16[128,512]{1,0:T(8,128)(2,1)S(1)} %get-tuple-element.180), channel_id=1, replica_groups=mesh['dp'=2,'expert'=32,'tensor'=4] {'tensor'}, dimensions={1}, use_global_device_ids=true | all-gather | bytes 655360 | tf_op jit(solution)/shard_map/all_gather | solution.py:99
  341.6 5.0 gather_fusion.3
  346.7 6.3 reshape.138
  353.0 3.9 multiply_convert_fusion
  356.9 3.8 copy.3579
  360.7 92.3 %all_to_all.20 = bf16[2,32,14,2048]{3,0,2,1:T(2,128)(2,1)S(1)} all-to-all(bf16[2,32,14,2048]{3,0,2,1:T(2,128)(2,1)S(1)} %copy.3579), channel_id=1, replica_groups=mesh['dp'=2,'expert'=32,'tensor'=4] {'expert'}, dimensions={1} | all-to-all | bytes 7340032 | tf_op jit(solution)/shard_map/all_to_all | solution.py:20
  453.0 7.9 %multiply_convert_fusion.1 = (bf16[2,32,14,352]{3,1,2,0:T(8,128)(2,1)S(1)}, bf16[2,32,14,352]{3,1,2,0:T(8,128)(2,1)S(1)}) fusion(f32[2,32,14,352]{3,1,2,0:T(8,128)} %copy-done.16, f32[2,32,14,352]{3,1,2,0:T(8,128)} %get-tuple-element.255, bf16[2,352,2048]{2,1,0:T(8,128)(2,1)S(1)} %copy-done.6, bf16[2,32,14,2048]{3,0,2,1:T(2,128)(2,1)S(1)} %all_to_all.20), kind=kOutput, calls=%fused_computation.32 | convolution fusion | flops 1295945728 | bytes 10338304 | tf_op jit(solution)/shard_map/escd,efd->escf/dot_general | solution.py:104
  463.1 4.0 add_convert_fusion
  467.4 6.8 %fusion.4 = bf16[2,1,2048,352]{2,3,0,1:T(8,128)(2,1)S(1)} fusion(bf16[2,32,14,352]{3,1,2,0:T(8,128)(2,1)S(1)} %get-tuple-element.182, bf16[2,32,14,2048]{3,0,2,1:T(2,128)(2,1)} %all-to-all-done), kind=kOutput, calls=%fused_computation.17 | convolution fusion | flops 1293287424 | bytes 7184384 | tf_op jit(solution)/shard_map/escd,escf->edf/dot_general | solution.py:34
  474.2 6.8 %fusion.3 = bf16[2,1,2048,352]{2,3,0,1:T(8,128)(2,1)S(1)} fusion(bf16[2,32,14,352]{3,1,2,0:T(8,128)(2,1)S(1)} %copy-done.11, bf16[2,32,14,2048]{3,0,2,1:T(2,128)(2,1)} %all-to-all-done), kind=kOutput, calls=%fused_computation.16 | convolution fusion | flops 1293287424 | bytes 7184384 | tf_op jit(solution)/shard_map/escd,escf->edf/dot_general | solution.py:31
  485.1 8.3 %bitcast_convert_fusion = bf16[2,352,2048]{2,1,0:T(8,128)(2,1)} fusion(bf16[2,32,14,352]{3,1,2,0:T(8,128)(2,1)S(1)} %copy-done.9, bf16[2,32,14,2048]{3,0,2,1:T(2,128)(2,1)} %copy-done.2), kind=kOutput, calls=%fused_computation.9 | convolution fusion | flops 1293287424 | bytes 7184384 | tf_op jit(solution)/shard_map/escf,escd->efd/dot_general | solution.py:28
  493.5 13.3 %reduce-scatter.7.cloned.1.call-done = bf16[2,32,14,512]{3,1,2,0:T(8,128)(2,1)} async-done(((bf16[2,32,14,2048]{3,1,2,0:T(8,128)(2,1)}), bf16[2,32,14,512]{3,1,2,0:T(8,128)(2,1)}) %reduce-scatter.7.cloned.1.call-update) | async-done | bytes 917520 | tf_op jit(solution)/shard_map/reduce_scatter | solution.py:116
  514.4 10.3 %all-to-all-start.3 = ((bf16[32,2,1,14,512]{4,1,3,2,0:T(2,128)(2,1)}), bf16[32,2,1,14,512]{4,1,3,2,0:T(2,128)(2,1)S(1)}, u32[]{:S(2)}, u32[]{:S(2)}) async-start(bf16[32,2,1,14,512]{4,1,3,2,0:T(2,128)(2,1)} %copy.3643), calls=%async_computation.5 | async-start | bytes 1835008 | tf_op jit(solution)/shard_map/all_to_all | solution.py:14
  527.4 34.1 %all-to-all-done.3 = bf16[32,2,1,14,512]{4,1,3,2,0:T(2,128)(2,1)S(1)} async-done(((bf16[32,2,1,14,512]{4,1,3,2,0:T(2,128)(2,1)}), bf16[32,2,1,14,512]{4,1,3,2,0:T(2,128)(2,1)S(1)}, u32[]{:S(2)}, u32[]{:S(2)}) %all-to-all-start.3) | async-done | bytes 917536 | tf_op jit(solution)/shard_map/all_to_all | solution.py:14
  572.3 14.0 %all-reduce.2 = (f32[128]{0:T(128)}, f32[128,6]{1,0:T(8,128)}) all-reduce(f32[128]{0:T(128)S(1)} %multiply_reduce_fusion.3, f32[128,6]{1,0:T(8,128)} %multiply_reduce_fusion), channel_id=1, replica_groups=mesh['dp'=2,'expert'=32,'tensor'=4] {'tensor'}, use_global_device_ids=true, to_apply=%region_12.13 | all-reduce | flops 896 | bytes 7168 | tf_op jit(solution)/shard_map/psum | solution.py:126
  588.6 10.9 %all_gather.15 = bf16[128,2048]{1,0:T(8,128)(2,1)S(1)} all-gather(bf16[128,512]{1,0:T(8,128)(2,1)S(1)} %subtract_convert_fusion), channel_id=1, replica_groups=mesh['dp'=2,'expert'=32,'tensor'=4] {'tensor'}, dimensions={1}, use_global_device_ids=true | all-gather | bytes 655360 | tf_op jit(solution)/shard_map/all_gather | solution.py:134
  601.0 4.1 reduce-scatter.9.cloned.1.call-done
  605.1 3.7 copy.3649
  608.8 45.4 %reduce-scatter.11.cloned.1.call-done = bf16[2,352,1024]{2,1,0:T(8,128)(2,1)} async-done(((bf16[2,352,2048]{2,1,0:T(8,128)(2,1)}), bf16[2,352,1024]{2,1,0:T(8,128)(2,1)}) %reduce-scatter.11.cloned.1.call-update) | async-done | bytes 1441808 | tf_op jit(solution)/shard_map/reduce_scatter | solution.py:144
  (232 shorter events, 67.4 us)
Async XLA Ops:
  8.0 1.6 copy-start
  8.0 4.4 copy-start.14
  8.0 53.8 %all-reduce.5.cloned.1.call-start = ((), (), s32[]{:S(2)}) async-start(), calls=%async_computation.8 | async-start | bytes 1048576 | tf_op jit(solution)/shard_map/psum | solution.py:56
  11.7 50.1 %copy-start.7 = (bf16[128,2048]{1,0:T(8,128)(2,1)S(1)}, bf16[128,2048]{1,0:T(8,128)(2,1)}, u32[]{:S(2)}) copy-start(bf16[128,2048]{1,0:T(8,128)(2,1)} %param.10) | copy-start | bytes 1572868
  11.7 51.4 %copy-start.13 = (f32[2048]{0:T(1024)S(1)}, f32[2048]{0:T(1024)}, u32[]{:S(2)}) copy-start(f32[2048]{0:T(1024)} %param.12) | copy-start | bytes 24580
  11.8 85.8 %all-gather.3.cloned.1.call-start = ((), (), s32[]{:S(2)}) async-start(), calls=%async_computation.9 | async-start | bytes 8650752 | tf_op jit(solution)/shard_map/all_gather | solution.py:52
  84.2 128.9 %all-to-all-start = ((bf16[2,32,14,2048]{3,0,2,1:T(2,128)(2,1)}), bf16[2,32,14,2048]{3,0,2,1:T(2,128)(2,1)}, u32[]{:S(2)}, u32[]{:S(2)}) async-start(bf16[2,32,14,2048]{3,0,2,1:T(2,128)(2,1)} %copy.3511), calls=%async_computation | async-start | bytes 7340032 | tf_op jit(solution)/shard_map/all_to_all | solution.py:20
  96.7 132.8 %all-gather.5.cloned.1.call-start = ((), (), s32[]{:S(2)}) async-start(), calls=%async_computation.10 | async-start | bytes 4325376 | tf_op jit(solution)/shard_map/all_gather | solution.py:53
  97.2 177.4 %reduce-scatter.5.cloned.1.call-start = ((), (), s32[]{:S(2)}) async-start(), calls=%async_computation.11 | async-start | bytes 4587520 | tf_op jit(solution)/shard_map/reduce_scatter | solution.py:86
  213.1 8.6 %copy-start.1 = (bf16[2,2,2048,352]{2,3,1,0:T(8,128)(2,1)S(1)}, bf16[2,2,2048,352]{2,3,1,0:T(8,128)(2,1)}, u32[]{:S(2)}) copy-start(bf16[2,2,2048,352]{2,3,1,0:T(8,128)(2,1)} %all-gather.3.cloned.1.call-done) | copy-start | bytes 17301508
  220.6 1.2 copy-start.16
  229.5 5.9 copy-start.8
  274.6 4.1 copy-start.4
  280.4 12.8 %copy-start.15 = (f32[128,6]{0,1:T(8,128)S(1)}, f32[128,6]{0,1:T(8,128)}, u32[]{:S(2)}) copy-start(f32[128,6]{0,1:T(8,128)} %param.14) | copy-start | bytes 9220
  282.8 36.2 %all-to-all-start.1 = ((bf16[32,2,1,14,512]{4,1,3,2,0:T(2,128)(2,1)}), bf16[32,2,1,14,512]{4,1,3,2,0:T(2,128)(2,1)S(1)}, u32[]{:S(2)}, u32[]{:S(2)}) async-start(bf16[32,2,1,14,512]{4,1,3,2,0:T(2,128)(2,1)} %copy.3576), calls=%async_computation.2 | async-start | bytes 1835008 | tf_op jit(solution)/shard_map/all_to_all | solution.py:14
  293.1 213.6 %reduce-scatter.7.cloned.1.call-start = ((), (), s32[]{:S(2)}) async-start(), calls=%async_computation.12 | async-start | bytes 4587520 | tf_op jit(solution)/shard_map/reduce_scatter | solution.py:116
  324.8 4.8 copy-start.12
  360.7 92.3 %copy-start.6 = (bf16[2,352,2048]{2,1,0:T(8,128)(2,1)S(1)}, bf16[2,352,2048]{2,1,0:T(8,128)(2,1)}, u32[]{:S(2)}) copy-start(bf16[2,352,2048]{2,1,0:T(8,128)(2,1)} %all-gather.5.cloned.1.call-done) | copy-start | bytes 8650756
  360.7 100.2 %slice-start = ((s8[5767168]{0:T(1024)(128)(4,1)}), s8[4194304]{0:T(1024)(128)(4,1)S(1)}, s32[]{:S(2)}) async-start(s8[5767168]{0:T(1024)(128)(4,1)} %bitcast.269), calls=%async_computation.15 | async-start | bytes 8388608
  453.0 7.9 %copy-start.2 = (bf16[2,32,14,2048]{3,0,2,1:T(2,128)(2,1)}, bf16[2,32,14,2048]{3,0,2,1:T(2,128)(2,1)S(1)}, u32[]{:S(2)}) copy-start(bf16[2,32,14,2048]{3,0,2,1:T(2,128)(2,1)S(1)} %all_to_all.20) | copy-start | bytes 11010052
  453.0 7.9 %slice-start.1 = ((s8[5767168]{0:T(1024)(128)(4,1)}), s8[1572864]{0:T(1024)(128)(4,1)S(1)}, s32[]{:S(2)}) async-start(s8[5767168]{0:T(1024)(128)(4,1)} %bitcast.269), calls=%async_computation.16 | async-start | bytes 3145728
  460.9 2.1 copy-start.10
  467.1 138.0 %reduce-scatter.9.cloned.1.call-start = ((), (), s32[]{:S(2)}) async-start(), calls=%async_computation.13 | async-start | bytes 8650752 | tf_op jit(solution)/shard_map/reduce_scatter | solution.py:141
  467.4 6.8 %copy-start.11 = (bf16[2,32,14,352]{3,1,2,0:T(8,128)(2,1)S(1)}, bf16[2,32,14,352]{3,1,2,0:T(8,128)(2,1)}, u32[]{:S(2)}) copy-start(bf16[2,32,14,352]{3,1,2,0:T(8,128)(2,1)} %copy-done.10) | copy-start | bytes 1892356
  484.0 1.1 copy-start.9
  484.0 170.2 %reduce-scatter.11.cloned.1.call-start = ((), (), s32[]{:S(2)}) async-start(), calls=%async_computation.14 | async-start | bytes 4325376 | tf_op jit(solution)/shard_map/reduce_scatter | solution.py:144
  506.7 3.7 copy-start.3
  514.4 47.1 %all-to-all-start.3 = ((bf16[32,2,1,14,512]{4,1,3,2,0:T(2,128)(2,1)}), bf16[32,2,1,14,512]{4,1,3,2,0:T(2,128)(2,1)S(1)}, u32[]{:S(2)}, u32[]{:S(2)}) async-start(bf16[32,2,1,14,512]{4,1,3,2,0:T(2,128)(2,1)} %copy.3643), calls=%async_computation.5 | async-start | bytes 1835008 | tf_op jit(solution)/shard_map/all_to_all | solution.py:14
  567.4 4.8 copy-start.5
Sparse Core Ops, SparseCore 0:
  11.9 49.8 all-reduce.4
  235.6 38.9 reduce-scatter.4
  467.2 39.4 reduce-scatter.6
  509.1 95.9 reduce-scatter.8
  608.0 46.0 reduce-scatter.10
Sparse Core Ops, SparseCore 1:
  14.1 83.0 all-gather.2
  98.9 109.0 all-gather.4
